TPU v7x, 256 devices: a whole 4x4x8 slice. The times are simulated.
256 devices in a mesh: seq: 32 (over y, z), tensor: 8 (over x, core).
Axes of the slice: x: 4, y: 4, z: 8, core: 2. Of those that a mesh axis runs over, the one named last changes fastest.
Arguments:
- query: bfloat16 [4096, 2048], P('seq', 'tensor')
- suffix_kv: bfloat16 [4096, 4, 2, 128], P('seq'), may hold values from -6 to 6
- segment_ids: int32 [32, 128], P('seq'), may hold values from 0 to 3, never falling along the last dimension, each value on 1 to 64 neighbouring positions
- request_prefix: int32 [32, 4], P('seq'), may hold values from 0 to 3
- prefix_kv: bfloat16 [32768, 4, 2, 128], P('seq')
- shard_prefix: int32 [32], P('seq'), may hold values from 0 to 3, as said below
- residual: bfloat16 [4096, 2048], P('seq'), may hold values from -3.2 to 3.2
- out_weight: bfloat16 [2048, 2048], P('tensor'), may hold values from -0.1875 to 0.1875
- norm_gain: float32 [2048], replicated, may hold values from 0.1 to 1.9
- expert_ids: int32 [4096, 6], P('seq'), may hold values from 0 to 63, all different within a row; in each aligned block of 128 rows (0 to 127, 128 to 255, ...) at most 24 rows name the same one
- gate_weights: float32 [4096, 6], P('seq'), may hold values from 0.05 to 0.5
- expert_in: bfloat16 [64, 2048, 2, 1408], P('seq', None, None, 'tensor'), may hold values from -0.125 to 0.125
- expert_out: bfloat16 [64, 1408, 2048], P('seq', 'tensor'), may hold values from -0.21875 to 0.21875
Outputs:
- attended: bfloat16 [4096, 2048], P('seq', 'tensor')
- layer_out: bfloat16 [4096, 2048], P('seq', 'tensor')
Inputs may be any that keep to these rules, and one draw needn't show every extreme that they name: `segment_ids`: on each seq index the segment numbers never fall along the 128 positions and every number occurs. `shard_prefix`: every prefix owns the same number of shards. `expert_ids`: each row names 6 different experts; within the 128 rows of one seq index no expert is named more than 24 times, and that count is reached.
All inputs are finite; a program needn't handle non-finite values.
Results may differ from a plain program's by a relative error of at most 0.02.
Values may be sent and summed in bfloat16 or wider, within the bound.
No kernel may reach another device: no remote copies, remote signals or barrier semaphores. Data moves between devices by JAX's collectives and lax.ppermute only.
A program may use at most 128 MiB of HBM per device.

v0:
```python
import jax
import jax.numpy as jnp
from jax import lax
from jax.sharding import PartitionSpec as P

QH = 16
KVH = 4
NEG_FLOOR = -1e30


def fold_block(carried, queries, key_rows, values, allowed, score_scale):
    running_max, running_sum, weighted = carried
    scores = (
        jnp.einsum("rhd,kd->rhk", queries, key_rows, preferred_element_type=jnp.float32)
        * score_scale
    )
    scores = jnp.where(allowed[:, None, :], scores, -jnp.inf)
    new_max = jnp.maximum(running_max, jnp.max(scores, axis=2))
    weights = jnp.exp(scores - new_max[:, :, None])
    shrink = jnp.exp(running_max - new_max)
    gathered = jnp.einsum(
        "rhk,kd->rhd", weights.astype(jnp.bfloat16), values, preferred_element_type=jnp.float32
    )
    return (
        new_max,
        running_sum * shrink + jnp.sum(weights, axis=2),
        weighted * shrink[:, :, None] + gathered,
    )


def body(
    query,
    suffix_kv,
    segment_ids,
    request_prefix,
    prefix_kv,
    shard_prefix,
    residual,
    out_weight,
    norm_gain,
    expert_ids,
    gate_weights,
    expert_in,
    expert_out,
):
    tok_rows = query.shape[0]
    head_size = suffix_kv.shape[3]
    heads_here = query.shape[1] // head_size
    kv_head = lax.axis_index("tensor") * heads_here // (QH // KVH)
    score_scale = head_size ** (-0.5)
    queries = query.reshape(tok_rows, heads_here, head_size)
    segments = segment_ids[0]
    requests = jnp.arange(request_prefix.shape[1], dtype=jnp.int32)
    row_prefix = jnp.sum(
        jnp.where(segments[:, None] == requests[None, :], request_prefix[0][None, :], 0), axis=1
    )
    blank_state = (
        jnp.full((tok_rows, heads_here), NEG_FLOOR, jnp.float32),
        jnp.zeros((tok_rows, heads_here), jnp.float32),
        jnp.zeros((tok_rows, heads_here, head_size), jnp.float32),
    )
    shard_len = prefix_kv.shape[0]
    own_cache = lax.dynamic_slice_in_dim(prefix_kv, kv_head, 1, 1).reshape(shard_len, 2 * head_size)
    cache_rows = lax.all_gather(own_cache, "seq", axis=0, tiled=True)
    owners = lax.all_gather(shard_prefix, "seq", axis=0, tiled=True)
    shard_count = owners.shape[0]
    shards = cache_rows.reshape(shard_count, -1, 2, head_size)

    def one_shard(inner_state, shard_item):
        block_rows, shard_owner = shard_item
        matching = row_prefix == shard_owner

        def attend(current):
            allowed = jnp.broadcast_to(matching[:, None], (tok_rows, block_rows.shape[0]))
            return fold_block(
                current, queries, block_rows[:, 0], block_rows[:, 1], allowed, score_scale
            )

        return (lax.cond(jnp.any(matching), attend, lambda current: current, inner_state), None)

    final_state, unused = lax.scan(one_shard, blank_state, (shards, owners))
    carried = final_state
    own_suffix = lax.dynamic_slice_in_dim(suffix_kv, kv_head, 1, 1).reshape(tok_rows, 2, head_size)
    positions = jnp.arange(tok_rows)
    causal = (segments[:, None] == segments[None, :]) & (positions[None, :] <= positions[:, None])
    carried = fold_block(carried, queries, own_suffix[:, 0], own_suffix[:, 1], causal, score_scale)
    running_max, running_sum, weighted = carried
    attention = (
        (weighted / running_sum[:, :, None])
        .reshape(tok_rows, heads_here * head_size)
        .astype(jnp.bfloat16)
    )
    projected = jnp.dot(attention, out_weight, preferred_element_type=jnp.float32)
    model_width = residual.shape[1]
    slice_width = model_width // lax.axis_size("tensor")
    first_col = lax.axis_index("tensor") * slice_width
    shared = lax.psum_scatter(projected, "tensor", scatter_dimension=1, tiled=True)
    hidden_state = (
        lax.dynamic_slice_in_dim(residual, first_col, slice_width, 1).astype(jnp.float32) + shared
    )
    squares = lax.psum(jnp.sum(hidden_state * hidden_state, axis=1), "tensor")
    gain_cols = lax.dynamic_slice_in_dim(norm_gain, first_col, slice_width, 0)
    normed = (
        hidden_state * lax.rsqrt(squares / model_width + 1e-06)[:, None] * gain_cols[None, :]
    ).astype(jnp.bfloat16)
    attended = hidden_state.astype(jnp.bfloat16)
    exp_here = expert_in.shape[0]
    sources = lax.axis_size("seq")
    experts = exp_here * sources
    top_k = expert_ids.shape[1]
    capacity = 2 * tok_rows * top_k // experts
    flat_ids = expert_ids.reshape(-1)
    onehot = (flat_ids[:, None] == jnp.arange(experts, dtype=jnp.int32)[None, :]).astype(jnp.int32)
    slot_index = jnp.sum((jnp.cumsum(onehot, axis=0) - 1) * onehot, axis=1)
    places = flat_ids * capacity + slot_index
    outgoing = (
        jnp.zeros((experts * capacity, slice_width), jnp.bfloat16)
        .at[places]
        .set(jnp.repeat(normed, top_k, axis=0))
    )
    incoming = lax.all_to_all(
        outgoing.reshape(sources, exp_here, capacity, slice_width),
        "seq",
        split_axis=0,
        concat_axis=0,
        tiled=True,
    )
    gate_up = jnp.einsum(
        "sjcd,jdgh->sjcgh",
        lax.all_gather(incoming, "tensor", axis=3, tiled=True),
        expert_in,
        preferred_element_type=jnp.float32,
    )
    hidden = (jax.nn.silu(gate_up[:, :, :, 0]) * gate_up[:, :, :, 1]).astype(jnp.bfloat16)
    group_terms = jnp.einsum(
        "sjch,jhd->sjcd", hidden, expert_out, preferred_element_type=jnp.float32
    )
    expert_rows_out = lax.psum_scatter(
        group_terms.astype(jnp.bfloat16), "tensor", scatter_dimension=3, tiled=True
    )
    returned = lax.all_to_all(expert_rows_out, "seq", split_axis=0, concat_axis=0, tiled=True)
    picked = returned.reshape(experts * capacity, slice_width)[places].reshape(
        tok_rows, top_k, slice_width
    )
    mixture = jnp.sum(gate_weights[:, :, None] * picked.astype(jnp.float32), axis=1)
    layer_out = (hidden_state + mixture).astype(jnp.bfloat16)
    return (attended, layer_out)


def solution(mesh):
    in_specs = (
        P("seq", "tensor"),
        P("seq", None, None, None),
        P("seq", None),
        P("seq", None),
        P("seq", None, None, None),
        P("seq"),
        P("seq", None),
        P("tensor", None),
        P(),
        P("seq", None),
        P("seq", None),
        P("seq", None, None, "tensor"),
        P("seq", "tensor", None),
    )
    out_specs = (P("seq", "tensor"), P("seq", "tensor"))
    return jax.shard_map(body, mesh=mesh, in_specs=in_specs, out_specs=out_specs, check_vma=False)
```

profile of v0, /device:TPU:32, one launch (start us, length us, event | category | flops | bytes accessed | tf_op | source)
XLA Modules:
  0.0 573.5 jit_solution(9225628321920478958)
XLA Ops:
  14.0 23.0 %all-reduce = s32[32]{0:T(128)S(1)} all-reduce(s32[32]{0:T(128)S(1)} %dynamic-update-slice), channel_id=1, replica_groups=mesh['seq'=32,'tensor'=8] {'seq'}, use_global_device_ids=true, to_apply=%add | all-reduce | flops 32 | bytes 256
  37.4 113.8 %all-gather.3.cloned.1.call-done = bf16[32768,256]{0,1:T(8,128)(2,1)} async-done(((bf16[1024,256]{0,1:T(8,128)(2,1)}), bf16[32768,256]{0,1:T(8,128)(2,1)}) %all-gather.3.cloned.1.call-update) | async-done | bytes 16777232 | tf_op jit(solution)/shard_map/all_gather | solution.py:64
  151.2 18.7 %copy.104 = bf16[32,8,32,1024]{3,2,1,0:T(8,128)(2,1)} copy(bf16[32,8,32,1024]{3,1,2,0:T(8,128)(2,1)} %bitcast.106) | data formatting | bytes 33554432
  169.8 23.0 %copy.78 = bf16[32,1024,2,128]{3,1,2,0:T(8,128)(2,1)} copy(bf16[32,1024,2,128]{1,0,3,2:T(8,128)(2,1)} %bitcast.105) | data formatting | bytes 33554432 | tf_op jit(solution)/shard_map/while | solution.py:81
  192.9 111.5 %while.14 = (s32[]{:T(128)}, f32[128,2]{0,1:T(2,128)S(1)}, f32[128,2]{0,1:T(2,128)S(1)}, f32[128,2,128]{2,0,1:T(8,128)S(1)}, s32[32]{0:T(128)S(1)}, /*index=5*/s...) while((s32[]{:T(128)}, f32[128,2]{0,1:T(2,128)S(1)}, ...), condition=%wide.region_7.8_spmd, body=%wide.region_1.7_spmd.sunk | while | flops 136119040 | bytes 5064039 | solution.py:81
  195.3 2.0 conditional.2
  199.8 2.1 conditional.2
  209.2 2.0 conditional.2
  213.7 2.1 conditional.2
  223.2 2.0 conditional.2
  232.6 2.0 conditional.2
  239.6 2.1 conditional.2
  246.5 2.0 conditional.2
  253.5 2.1 conditional.2
  258.0 2.1 conditional.2
  274.4 2.1 conditional.2
  293.3 2.1 conditional.2
  297.8 2.1 conditional.2
  302.3 2.1 conditional.2
  304.8 2.6 fusion.39
  311.1 59.8 %reduce-scatter.3.cloned.1.call-done = f32[128,256]{1,0:T(8,128)} async-done(((f32[128,2048]{1,0:T(8,128)}), f32[128,256]{1,0:T(8,128)}) %reduce-scatter.3.cloned.1.call-update) | async-done | bytes 131088 | tf_op jit(solution)/shard_map/reduce_scatter | solution.py:97
  371.9 12.9 %psum.7 = f32[128]{0:T(128)S(1)} all-reduce(f32[128]{0:T(128)S(1)} %multiply_reduce_fusion.1), channel_id=1, replica_groups=mesh['seq'=32,'tensor'=8] {'tensor'}, use_global_device_ids=true, to_apply=%region_15.16 | all-reduce | flops 128 | bytes 1024 | tf_op jit(solution)/shard_map/psum | solution.py:101
  386.8 6.7 %scatter_custom_fusion = bf16[1536,256]{1,0:T(8,128)(2,1)} fusion(s32[768]{0:T(1024)S(1)} %fusion.33, bf16[768,256]{1,0:T(8,128)(2,1)} %reshape.146, bf16[]{:T(256)} %constant.72.clone.1), kind=kCustom, calls=%fused_computation.34 | custom fusion | bytes 786944 | tf_op jit(solution)/shard_map/scatter | solution.py:119
  393.5 32.7 %all_to_all.10 = bf16[32,2,24,256]{3,2,1,0:T(8,128)(2,1)S(1)} all-to-all(bf16[32,2,24,256]{3,2,1,0:T(8,128)(2,1)} %bitcast.107), channel_id=1, replica_groups=mesh['seq'=32,'tensor'=8] {'seq'}, dimensions={0} | all-to-all | bytes 1572864 | tf_op jit(solution)/shard_map/all_to_all | solution.py:121
  427.4 40.6 %all-gather.5.cloned.1.call-done = bf16[32,2,24,2048]{3,2,0,1:T(8,128)(2,1)} async-done(((bf16[32,2,24,256]{3,2,0,1:T(8,128)(2,1)}), bf16[32,2,24,2048]{3,2,0,1:T(8,128)(2,1)}) %all-gather.5.cloned.1.call-update) | async-done | bytes 6291472 | tf_op jit(solution)/shard_map/all_gather | solution.py:130
  468.0 5.7 fusion.9
  473.7 4.6 convert_bitcast_fusion
  478.3 46.1 %reduce-scatter.5.cloned.1.call-done = bf16[32,2,24,256]{3,2,0,1:T(8,128)(2,1)} async-done(((bf16[32,2,24,2048]{3,2,0,1:T(8,128)(2,1)}), bf16[32,2,24,256]{3,2,0,1:T(8,128)(2,1)}) %reduce-scatter.5.cloned.1.call-update) | async-done | bytes 786448 | tf_op jit(solution)/shard_map/reduce_scatter | solution.py:138
  524.4 2.1 copy.92
  526.5 10.1 %all-to-all-start.1 = ((bf16[32,2,24,256]{3,2,1,0:T(8,128)(2,1)}), bf16[32,2,24,256]{3,2,1,0:T(8,128)(2,1)}, u32[]{:S(2)}, u32[]{:S(2)}) async-start(bf16[32,2,24,256]{3,2,1,0:T(8,128)(2,1)} %copy.92), calls=%async_computation.3 | async-start | bytes 1572864 | tf_op jit(solution)/shard_map/all_to_all | solution.py:141
  536.8 22.6 %all-to-all-done.1 = bf16[32,2,24,256]{3,2,1,0:T(8,128)(2,1)} async-done(((bf16[32,2,24,256]{3,2,1,0:T(8,128)(2,1)}), bf16[32,2,24,256]{3,2,1,0:T(8,128)(2,1)}, u32[]{:S(2)}, u32[]{:S(2)}) %all-to-all-start.1) | async-done | bytes 786464 | tf_op jit(solution)/shard_map/all_to_all | solution.py:141
  559.3 3.4 gather_fusion
  (262 shorter events, 115.0 us)
Async XLA Ops:
  7.2 460.8 %copy-start = (bf16[2,2048,2,176]{1,3,2,0:T(8,128)(2,1)S(1)}, bf16[2,2048,2,176]{1,3,2,0:T(8,128)(2,1)}, u32[]{:S(2)}) copy-start(bf16[2,2048,2,176]{1,3,2,0:T(8,128)(2,1)} %param.28) | copy-start | bytes 8650756
  7.2 5.5 copy-start.7
  7.2 29.8 %copy-start.4 = (s32[1,128]{1,0:T(1,128)S(1)}, s32[1,128]{1,0:T(1,128)}, u32[]{:S(2)}) copy-start(s32[1,128]{1,0:T(1,128)} %param.19) | copy-start | bytes 1540
  7.2 29.8 %copy-start.6 = (s32[1,4]{1,0:T(1,128)S(1)}, s32[1,4]{1,0:T(1,128)}, u32[]{:S(2)}) copy-start(s32[1,4]{1,0:T(1,128)} %param.20) | copy-start | bytes 52
  7.2 144.0 %all-gather.3.cloned.1.call-start = ((), (), s32[]{:S(2)}) async-start(), calls=%async_computation.4 | async-start | bytes 17301504 | tf_op jit(solution)/shard_map/all_gather | solution.py:64
  10.0 360.9 %reduce-scatter.3.cloned.1.call-start = ((), (), s32[]{:S(2)}) async-start(), calls=%async_computation.5 | async-start | bytes 1179648 | tf_op jit(solution)/shard_map/reduce_scatter | solution.py:97
  304.4 3.0 copy-start.2
  307.4 160.7 %all-gather.5.cloned.1.call-start = ((), (), s32[]{:S(2)}) async-start(), calls=%async_computation.6 | async-start | bytes 7077888 | tf_op jit(solution)/shard_map/all_gather | solution.py:130
  427.2 97.2 %reduce-scatter.5.cloned.1.call-start = ((), (), s32[]{:S(2)}) async-start(), calls=%async_computation.7 | async-start | bytes 7077888 | tf_op jit(solution)/shard_map/reduce_scatter | solution.py:138
  468.0 5.7 copy-start.5
  478.3 58.4 %copy-start.3 = (f32[128,6]{0,1:T(8,128)S(1)}, f32[128,6]{0,1:T(8,128)}, u32[]{:S(2)}) copy-start(f32[128,6]{0,1:T(8,128)} %param.27) | copy-start | bytes 9220
  526.5 32.8 %all-to-all-start.1 = ((bf16[32,2,24,256]{3,2,1,0:T(8,128)(2,1)}), bf16[32,2,24,256]{3,2,1,0:T(8,128)(2,1)}, u32[]{:S(2)}, u32[]{:S(2)}) async-start(bf16[32,2,24,256]{3,2,1,0:T(8,128)(2,1)} %copy.92), calls=%async_computation.3 | async-start | bytes 1572864 | tf_op jit(solution)/shard_map/all_to_all | solution.py:141
  559.3 6.1 %copy-start.1 = (f32[128,256]{1,0:T(8,128)S(1)}, f32[128,256]{1,0:T(8,128)}, u32[]{:S(2)}) copy-start(f32[128,256]{1,0:T(8,128)} %reduce-scatter.3.cloned.1.call-done) | copy-start | bytes 393220
Sparse Core Ops, SparseCore 0:
  10.6 140.5 all-gather.2
  307.5 63.3 reduce-scatter.2
  427.3 40.6 all-gather.4
  478.4 45.9 reduce-scatter.4
where the time goes:
time: 577 us; the launch traced here: 573 us
  waiting for transfers between devices  283 us (49%)
  local copies, waits for them, and re-layouts  101 us (18%)
  blocking collectives  68.6 us (12%)
  other arithmetic  51 us (9%)
  matrix products  25 us (4%)
  loops' own time  19.9 us (3%)
  between operations  14.7 us (3%)
  starting transfers between devices  10.5 us (2%)
    all_gather x1, waiting for transfers between devices, body(): cache_rows = lax.all_gather(own_cache, 'seq', axis=0, tiled=True)  114 us
    reduce_scatter x1, waiting for transfers between devices, body(): lax.psum_scatter(projected, 'tensor', scatter_dimension=1, tiled=True)  59.8 us
    reduce_scatter x1, waiting for transfers between devices, body(): lax.psum_scatter(group_terms.astype(jnp.bfloat16), 'tensor', scatter_dime...  46.1 us
    reduce_or x32, other arithmetic, one_shard(): jnp.any(matching)  40.7 us
    all_gather x1, waiting for transfers between devices, body(): lax.all_gather(incoming, 'tensor', axis=3, tiled=True)  40.6 us
    all_to_all x1, blocking collectives, body(): lax.all_to_all(outgoing.reshape(sources, exp_here, capacity, slice_width)...  32.7 us
    while x3, local copies, waits for them, and re-layouts, body(): final_state, unused = lax.scan(one_shard, blank_state, (shards, owners))  23.2 us
    unnamed x1, blocking collectives  23 us
  transfers between devices with their start and end apart: 5, of which 5 were waited for; matrix products, arithmetic and copies ran while one was open for 1% of the time, Pallas kernels for 0%

commit v1 on v0

--- a/solution.py
+++ b/solution.py
@@ -127,7 +127,15 @@
     )
     gate_up = jnp.einsum(
         "sjcd,jdgh->sjcgh",
-        lax.all_gather(incoming, "tensor", axis=3, tiled=True),
+        jnp.concatenate(
+            lax.all_to_all(
+                jnp.stack([incoming] * lax.axis_size("tensor"), axis=0),
+                axis_name="tensor",
+                split_axis=0,
+                concat_axis=0,
+            ),
+            3,
+        ),
         expert_in,
         preferred_element_type=jnp.float32,
     )

time: 577 us -> 624 us (1.081)
  blocking collectives: 68.6 us -> 143 us
  waiting for transfers between devices: 283 us -> 236 us
  local copies, waits for them, and re-layouts: 101 us -> 121 us
    all_to_all x0 -> x1, blocking collectives: none -> 74.7 us  [body(): lax.all_to_all(jnp.stack([incoming] * lax.axis_size('tensor'), axis=0), a...]
    all_gather x1 -> x0, waiting for transfers between devices: 40.6 us -> none  [body(): lax.all_gather(incoming, 'tensor', axis=3, tiled=True)]
    reshape x0 -> x2, local copies, waits for them, and re-layouts: none -> 20.1 us  [body(): jnp.concatenate(lax.all_to_all(jnp.stack([incoming] * lax.axis_size('tens...]
    reduce_scatter x1, waiting for transfers between devices: 46.1 us -> 39.7 us  [body(): lax.psum_scatter(group_terms.astype(jnp.bfloat16), 'tensor', scatter_dime...]
  transfers between devices with their start and end apart: 5 -> 4, of which waited for: 5 -> 4; matrix products, arithmetic and copies ran while one was open for 1% -> 1% of each run, Pallas kernels for 0% -> 0%
where the time goes in v1:
time: 624 us; the launch traced here: 621 us
  waiting for transfers between devices  236 us (38%)
  blocking collectives  143 us (23%)
  local copies, waits for them, and re-layouts  121 us (19%)
  other arithmetic  51 us (8%)
  matrix products  25 us (4%)
  loops' own time  19.9 us (3%)
  between operations  14.7 us (2%)
  starting transfers between devices  10.3 us (2%)
    all_gather x1, waiting for transfers between devices, body(): cache_rows = lax.all_gather(own_cache, 'seq', axis=0, tiled=True)  114 us
    all_to_all x1, blocking collectives, body(): lax.all_to_all(jnp.stack([incoming] * lax.axis_size('tensor'), axis=0), a...  74.7 us
    reduce_scatter x1, waiting for transfers between devices, body(): lax.psum_scatter(projected, 'tensor', scatter_dimension=1, tiled=True)  59.8 us
    reduce_or x32, other arithmetic, one_shard(): jnp.any(matching)  40.7 us
    reduce_scatter x1, waiting for transfers between devices, body(): lax.psum_scatter(group_terms.astype(jnp.bfloat16), 'tensor', scatter_dime...  39.7 us
    all_to_all x1, blocking collectives, body(): lax.all_to_all(outgoing.reshape(sources, exp_here, capacity, slice_width)...  32.7 us
    while x3, local copies, waits for them, and re-layouts, body(): final_state, unused = lax.scan(one_shard, blank_state, (shards, owners))  23.2 us
    unnamed x1, blocking collectives  23 us
  transfers between devices with their start and end apart: 4, of which 4 were waited for; matrix products, arithmetic and copies ran while one was open for 1% of the time, Pallas kernels for 0%

profile of v1, /device:TPU:32, one launch (start us, length us, event | category | flops | bytes accessed | tf_op | source)
XLA Modules:
  0.0 620.7 jit_solution(17263645362288191511)
XLA Ops:
  14.0 23.0 %all-reduce = s32[32]{0:T(128)S(1)} all-reduce(s32[32]{0:T(128)S(1)} %dynamic-update-slice), channel_id=1, replica_groups=mesh['seq'=32,'tensor'=8] {'seq'}, use_global_device_ids=true, to_apply=%add | all-reduce | flops 32 | bytes 256
  37.4 113.8 %all-gather.2.cloned.1.call-done = bf16[32768,256]{0,1:T(8,128)(2,1)} async-done(((bf16[1024,256]{0,1:T(8,128)(2,1)}), bf16[32768,256]{0,1:T(8,128)(2,1)}) %all-gather.2.cloned.1.call-update) | async-done | bytes 16777232 | tf_op jit(solution)/shard_map/all_gather | solution.py:64
  151.2 18.7 %copy.106 = bf16[32,8,32,1024]{3,2,1,0:T(8,128)(2,1)} copy(bf16[32,8,32,1024]{3,1,2,0:T(8,128)(2,1)} %bitcast.110) | data formatting | bytes 33554432
  169.8 23.0 %copy.79 = bf16[32,1024,2,128]{3,1,2,0:T(8,128)(2,1)} copy(bf16[32,1024,2,128]{1,0,3,2:T(8,128)(2,1)} %bitcast.108) | data formatting | bytes 33554432 | tf_op jit(solution)/shard_map/while | solution.py:81
  192.9 111.5 %while.14 = (s32[]{:T(128)}, f32[128,2]{0,1:T(2,128)S(1)}, f32[128,2]{0,1:T(2,128)S(1)}, f32[128,2,128]{2,0,1:T(8,128)S(1)}, s32[32]{0:T(128)S(1)}, /*index=5*/s...) while((s32[]{:T(128)}, f32[128,2]{0,1:T(2,128)S(1)}, ...), condition=%wide.region_7.8_spmd, body=%wide.region_1.7_spmd.sunk | while | flops 136119040 | bytes 5064039 | solution.py:81
  199.8 2.1 conditional.2
  209.2 2.0 conditional.2
  213.7 2.1 conditional.2
  232.6 2.0 conditional.2
  239.6 2.1 conditional.2
  246.5 2.0 conditional.2
  253.5 2.1 conditional.2
  258.0 2.1 conditional.2
  274.4 2.1 conditional.2
  293.3 2.1 conditional.2
  297.8 2.1 conditional.2
  302.3 2.1 conditional.2
  304.8 2.6 fusion.39
  311.1 59.8 %reduce-scatter.3.cloned.1.call-done = f32[128,256]{1,0:T(8,128)} async-done(((f32[128,2048]{1,0:T(8,128)}), f32[128,256]{1,0:T(8,128)}) %reduce-scatter.3.cloned.1.call-update) | async-done | bytes 131088 | tf_op jit(solution)/shard_map/reduce_scatter | solution.py:97
  371.9 12.9 %psum.7 = f32[128]{0:T(128)S(1)} all-reduce(f32[128]{0:T(128)S(1)} %multiply_reduce_fusion.1), channel_id=1, replica_groups=mesh['seq'=32,'tensor'=8] {'tensor'}, use_global_device_ids=true, to_apply=%region_15.16 | all-reduce | flops 128 | bytes 1024 | tf_op jit(solution)/shard_map/psum | solution.py:101
  386.8 6.7 %scatter_custom_fusion = bf16[1536,256]{1,0:T(8,128)(2,1)} fusion(s32[768]{0:T(1024)S(1)} %fusion.33, bf16[768,256]{1,0:T(8,128)(2,1)} %reshape.156, bf16[]{:T(256)} %constant.72.clone.1), kind=kCustom, calls=%fused_computation.34 | custom fusion | bytes 786944 | tf_op jit(solution)/shard_map/scatter | solution.py:119
  393.5 32.7 %all_to_all.15 = bf16[32,2,24,256]{3,2,1,0:T(8,128)(2,1)S(1)} all-to-all(bf16[32,2,24,256]{3,2,1,0:T(8,128)(2,1)} %bitcast.111), channel_id=1, replica_groups=mesh['seq'=32,'tensor'=8] {'seq'}, dimensions={0} | all-to-all | bytes 1572864 | tf_op jit(solution)/shard_map/all_to_all | solution.py:121
  426.9 74.7 %all_to_all.16 = bf16[8,32,2,24,256]{4,3,1,2,0:T(8,128)(2,1)S(1)} all-to-all(bf16[8,32,2,24,256]{4,3,1,2,0:T(8,128)(2,1)S(1)} %stack.2), channel_id=1, replica_groups=mesh['seq'=32,'tensor'=8] {'tensor'}, dimensions={0} | all-to-all | bytes 12582912 | tf_op jit(solution)/shard_map/all_to_all | solution.py:131
  501.6 9.6 %copy.92 = bf16[32,2,24,8,256]{4,3,2,0,1:T(8,128)(2,1)} copy(bf16[32,2,24,8,256]{4,2,0,1,3:T(8,128)(2,1)S(1)} %bitcast.109) | data formatting | bytes 12582912 | tf_op jit(solution)/shard_map/reshape | solution.py:130
  511.2 10.5 %reshape.169 = bf16[32,2,24,2048,1]{3,2,0,1,4:T(8,128)(2,1)} reshape(bf16[32,2,24,8,256]{4,3,2,0,1:T(8,128)(2,1)} %copy.92) | data formatting | bytes 12582912 | tf_op jit(solution)/shard_map/reshape | solution.py:130
  521.7 5.7 fusion.9
  527.4 4.6 convert_bitcast_fusion
  532.0 39.7 %reduce-scatter.5.cloned.1.call-done = bf16[32,2,24,256]{3,2,0,1:T(8,128)(2,1)} async-done(((bf16[32,2,24,2048]{3,2,0,1:T(8,128)(2,1)}), bf16[32,2,24,256]{3,2,0,1:T(8,128)(2,1)}) %reduce-scatter.5.cloned.1.call-update) | async-done | bytes 786448 | tf_op jit(solution)/shard_map/reduce_scatter | solution.py:146
  571.6 2.1 copy.94
  573.7 10.2 %all-to-all-start.2 = ((bf16[32,2,24,256]{3,2,1,0:T(8,128)(2,1)}), bf16[32,2,24,256]{3,2,1,0:T(8,128)(2,1)}, u32[]{:S(2)}, u32[]{:S(2)}) async-start(bf16[32,2,24,256]{3,2,1,0:T(8,128)(2,1)} %copy.94), calls=%async_computation.4 | async-start | bytes 1572864 | tf_op jit(solution)/shard_map/all_to_all | solution.py:149
  584.0 22.6 %all-to-all-done.2 = bf16[32,2,24,256]{3,2,1,0:T(8,128)(2,1)} async-done(((bf16[32,2,24,256]{3,2,1,0:T(8,128)(2,1)}), bf16[32,2,24,256]{3,2,1,0:T(8,128)(2,1)}, u32[]{:S(2)}, u32[]{:S(2)}) %all-to-all-start.2) | async-done | bytes 786464 | tf_op jit(solution)/shard_map/all_to_all | solution.py:149
  606.6 3.4 gather_fusion
  (263 shorter events, 118.5 us)
Async XLA Ops:
  7.2 514.5 %copy-start = (bf16[2,2048,2,176]{1,3,2,0:T(8,128)(2,1)S(1)}, bf16[2,2048,2,176]{1,3,2,0:T(8,128)(2,1)}, u32[]{:S(2)}) copy-start(bf16[2,2048,2,176]{1,3,2,0:T(8,128)(2,1)} %param.28) | copy-start | bytes 8650756
  7.2 5.5 copy-start.7
  7.2 29.8 %copy-start.4 = (s32[1,128]{1,0:T(1,128)S(1)}, s32[1,128]{1,0:T(1,128)}, u32[]{:S(2)}) copy-start(s32[1,128]{1,0:T(1,128)} %param.19) | copy-start | bytes 1540
  7.2 29.8 %copy-start.6 = (s32[1,4]{1,0:T(1,128)S(1)}, s32[1,4]{1,0:T(1,128)}, u32[]{:S(2)}) copy-start(s32[1,4]{1,0:T(1,128)} %param.20) | copy-start | bytes 52
  7.2 144.0 %all-gather.2.cloned.1.call-start = ((), (), s32[]{:S(2)}) async-start(), calls=%async_computation.5 | async-start | bytes 17301504 | tf_op jit(solution)/shard_map/all_gather | solution.py:64
  10.0 360.9 %reduce-scatter.3.cloned.1.call-start = ((), (), s32[]{:S(2)}) async-start(), calls=%async_computation.6 | async-start | bytes 1179648 | tf_op jit(solution)/shard_map/reduce_scatter | solution.py:97
  304.4 3.0 copy-start.2
  307.4 264.3 %reduce-scatter.5.cloned.1.call-start = ((), (), s32[]{:S(2)}) async-start(), calls=%async_computation.7 | async-start | bytes 7077888 | tf_op jit(solution)/shard_map/reduce_scatter | solution.py:146
  521.7 5.7 copy-start.5
  531.9 51.9 %copy-start.3 = (f32[128,6]{0,1:T(8,128)S(1)}, f32[128,6]{0,1:T(8,128)}, u32[]{:S(2)}) copy-start(f32[128,6]{0,1:T(8,128)} %param.27) | copy-start | bytes 9220
  573.7 32.9 %all-to-all-start.2 = ((bf16[32,2,24,256]{3,2,1,0:T(8,128)(2,1)}), bf16[32,2,24,256]{3,2,1,0:T(8,128)(2,1)}, u32[]{:S(2)}, u32[]{:S(2)}) async-start(bf16[32,2,24,256]{3,2,1,0:T(8,128)(2,1)} %copy.94), calls=%async_computation.4 | async-start | bytes 1572864 | tf_op jit(solution)/shard_map/all_to_all | solution.py:149
  606.6 6.1 copy-start.1
Sparse Core Ops, SparseCore 0:
  10.6 140.5 all-gather.1
  307.5 63.3 reduce-scatter.2
  532.1 39.5 reduce-scatter.4
